TPU v7x, 512 devices: a whole 4x8x8 slice. The times are simulated.
512 devices in a mesh: dp: 16 (over x_lo, y), space: 32 (over x_hi, z, core).
Axes of the slice: x: 4 (x_hi: 2, x_lo: 2; x = x_hi * 2 + x_lo), y: 8, z: 8, core: 2. Of those that a mesh axis runs over, the one named last changes fastest.
Arguments:
- inputs: bfloat16 [16, 10, 64, 32, 128], P('dp', None, 'space'), may hold values from -8 to 8
- land_mask: int32 [16, 10, 64, 32], P('dp', None, 'space'), may hold values 0 or 1
- weight_one: float32 [128, 27, 128], P('dp'), may hold values from -0.109375 to 0.109375
- weight_two: float32 [128, 27, 128], P('dp'), may hold values from -0.109375 to 0.109375
- cotangent: bfloat16 [16, 10, 64, 32, 128], P('dp', None, 'space'), may hold values from -6 to 6
Outputs:
- prediction: bfloat16 [16, 10, 64, 32, 128], P('dp', None, 'space')
- input_grad: bfloat16 [16, 10, 64, 32, 128], P('dp', None, 'space')
- grad_one: float32 [128, 27, 128], P('dp')
- grad_two: float32 [128, 27, 128], P('dp')
All inputs are finite; a program needn't handle non-finite values. No bound on the sum of `land_mask` on one device may be relied on, other than what follows from the above.
Results may differ from a plain program's by a relative error of at most 0.0067.
Values may be sent and summed in bfloat16 or wider, within the bound.
No kernel may reach another device: no remote copies, remote signals or barrier semaphores. Data moves between devices by JAX's collectives and lax.ppermute only.
A program may use at most 64 MiB of HBM per device.

v0:
```python
import jax
import jax.numpy as jnp
from jax import lax
from jax.sharding import PartitionSpec as P


def with_halo(cells, sides, width):
    for axis, dim in sides:
        count = lax.axis_size(axis)
        ends = count - 1
        head = lax.slice_in_dim(cells, 0, width, axis=dim)
        tail = lax.slice_in_dim(cells, cells.shape[dim] - width, cells.shape[dim], axis=dim)
        cells = jnp.concatenate(
            [
                lax.ppermute(tail, axis, [(i, (i + 1) % count) for i in range(ends)]),
                cells,
                lax.ppermute(head, axis, [((i + 1) % count, i) for i in range(ends)]),
            ],
            axis=dim,
        )
    return cells


def widen(field):
    rimmed = with_halo(field, (("space", 2),), 1)
    return jnp.pad(rimmed, ((0, 0), (1, 1), (0, 0), (1, 1), (0, 0)))


def group_window(padded, depth_off, mirrored, shape):
    depth, rows, columns = shape
    pieces = []
    for row_off in range(3):
        for col_off in range(3):
            row_at = 2 - row_off if mirrored else row_off
            col_at = 2 - col_off if mirrored else col_off
            piece = padded[
                :,
                depth_off : depth_off + depth,
                row_at : row_at + rows,
                col_at : col_at + columns,
                :,
            ]
            pieces.append(piece.reshape(-1, padded.shape[4]))
    return jnp.concatenate(pieces, axis=1)


def conv_full(padded, kernel, shape):
    channel = kernel.shape[0]
    total = None
    for group in range(3):
        window = group_window(padded, group, False, shape)
        block = jnp.transpose(kernel[:, 9 * group : 9 * group + 9, :], (1, 0, 2)).reshape(
            9 * channel, kernel.shape[2]
        )
        term = jnp.dot(window, block, preferred_element_type=jnp.float32)
        total = term if total is None else total + term
    return total


def transpose_part(padded, kernel, shape):
    channel = kernel.shape[0]
    total = None
    for group in range(3):
        window = group_window(padded, 2 - group, True, shape)
        block = kernel[:, 9 * group : 9 * group + 9, :].reshape(channel, 9 * kernel.shape[2])
        term = lax.dot_general(
            window, block, (((1,), (1,)), ((), ())), preferred_element_type=jnp.float32
        )
        total = term if total is None else total + term
    return total


def local_grad(padded, back_flat, shape):
    channel = padded.shape[4]
    terms = []
    for group in range(3):
        window = group_window(padded, group, False, shape)
        block = lax.dot_general(
            window, back_flat, (((0,), (0,)), ((), ())), preferred_element_type=jnp.float32
        )
        terms.append(jnp.transpose(block.reshape(9, channel, back_flat.shape[1]), (1, 0, 2)))
    return jnp.concatenate(terms, axis=1)


def kernel_again(kernel):
    return lax.all_gather(kernel, "dp", axis=0, tiled=True)


def reduce_grad(grad_full):
    owned = lax.psum_scatter(grad_full, "dp", scatter_dimension=0, tiled=True)
    return lax.psum(owned, "space")


def on_device(inputs, land_mask, weight_one, weight_two, cotangent):
    samples, depth, rows, columns, channel = inputs.shape
    shape = (depth, rows, columns)
    kernel_one = weight_one.astype(jnp.bfloat16)
    kernel_two = weight_two.astype(jnp.bfloat16)
    scale = land_mask.reshape(-1, 1).astype(jnp.float32)
    in_pad = widen(inputs)
    pre_one = conv_full(in_pad, kernel_again(kernel_one), shape)
    act_one = (scale * jax.nn.silu(pre_one)).astype(jnp.bfloat16).reshape(inputs.shape)
    act_pad = widen(act_one)
    pre_two = conv_full(act_pad, kernel_again(kernel_two), shape)
    prediction = (scale * pre_two).astype(jnp.bfloat16).reshape(inputs.shape)
    back_two = (cotangent.reshape(-1, channel).astype(jnp.float32) * scale).astype(jnp.bfloat16)
    back_pad = widen(back_two.reshape(inputs.shape))
    grad_two = reduce_grad(local_grad(act_pad, back_two, shape))
    pull_one = transpose_part(back_pad, kernel_again(kernel_two), shape)
    sigma = jax.nn.sigmoid(pre_one)
    back_one = (pull_one * scale * sigma * (1.0 + pre_one * (1.0 - sigma))).astype(jnp.bfloat16)
    first_pad = widen(back_one.reshape(inputs.shape))
    grad_one = reduce_grad(local_grad(in_pad, back_one, shape))
    pulled = transpose_part(first_pad, kernel_again(kernel_one), shape)
    input_grad = pulled.astype(jnp.bfloat16).reshape(inputs.shape)
    return (prediction, input_grad, grad_one, grad_two)


def solution(mesh):
    in_specs = (
        P("dp", None, "space", None, None),
        P("dp", None, "space", None),
        P("dp", None, None),
        P("dp", None, None),
        P("dp", None, "space", None, None),
    )
    out_specs = (
        P("dp", None, "space", None, None),
        P("dp", None, "space", None, None),
        P("dp", None, None),
        P("dp", None, None),
    )
    return jax.shard_map(
        on_device, mesh=mesh, in_specs=in_specs, out_specs=out_specs, check_vma=False
    )
```

profile of v0, /device:TPU:1, one launch (start us, length us, event | category | flops | bytes accessed | tf_op | source)
XLA Modules:
  0.0 553.1 jit_solution(8356080933103198237)
XLA Ops:
  9.0 5.4 collective-permute-start.4
  14.4 4.7 collective-permute-start.5
  20.1 1.9 collective-permute-start
  22.0 2.4 collective-permute-start.1
  26.2 31.4 %all_gather.9 = bf16[128,27,128]{2,0,1:T(8,128)(2,1)S(1)} all-gather(bf16[8,27,128]{2,0,1:T(8,128)(2,1)S(1)} %convert_element_type.56), channel_id=1, replica_groups=mesh['dp'=16,'space'=32] {'dp'}, dimensions={0}, use_global_device_ids=true | all-gather | bytes 940032 | tf_op jit(solution)/shard_map/all_gather | solution.py:86
  57.7 28.5 %all_gather.8 = bf16[128,27,128]{2,0,1:T(8,128)(2,1)S(1)} all-gather(bf16[8,27,128]{2,0,1:T(8,128)(2,1)S(1)} %convert_element_type.54), channel_id=1, replica_groups=mesh['dp'=16,'space'=32] {'dp'}, dimensions={0}, use_global_device_ids=true | all-gather | bytes 940032 | tf_op jit(solution)/shard_map/all_gather | solution.py:86
  103.9 17.2 %collective-permute-start.2 = (bf16[1,10,1,32,128]{4,3,2,1,0:T(8,128)(2,1)S(1)}, bf16[1,10,1,32,128]{4,3,2,1,0:T(8,128)(2,1)S(1)}, u32[]{:S(2)}, u32[]{:S(2)}) collective-permute-start(bf16[1,10,1,32,128]{4,3,2,1,0:T(8,128)(2,1)S(1)} %get-tuple-element.118), channel_id=1, source_target_pairs={{0,1},{1,2},{2,3},{3,4},{4,5},{5,6},{6,7},{7,8},{8,9},{9,10},{10,1... | collective-permute-start | bytes 245768 | tf_op jit(solution)/shard_map/ppermute | solution.py:15
  121.1 1.9 collective-permute-start.3
  124.5 3.6 collective-permute-start.6
  128.1 2.1 collective-permute-start.7
  135.1 1.8 fusion.20
  141.9 1.7 copy.66
  143.6 1.7 copy.65
  145.3 1.7 copy.64
  147.0 1.7 copy.63
  167.2 3.7 copy.73
  170.8 1.7 constant_dynamic-update-slice_fusion.89
  182.0 1.8 constant_dynamic-update-slice_fusion.88
  183.8 1.7 constant_dynamic-update-slice_fusion.87
  185.5 1.7 constant_dynamic-update-slice_fusion.86
  187.1 1.7 constant_dynamic-update-slice_fusion.85
  196.6 2.0 convolution_add_fusion.5
  200.5 68.5 %reduce-scatter.5.cloned.1.call-done = f32[8,27,128]{2,0,1:T(8,128)} async-done(((f32[128,27,128]{2,0,1:T(8,128)}), f32[8,27,128]{2,0,1:T(8,128)}) %reduce-scatter.5.cloned.1.call-update) | async-done | bytes 110608 | tf_op jit(solution)/shard_map/reduce_scatter | solution.py:90
  270.2 273.3 %all-reduce.7.cloned.1.call-done = (f32[8,27,128]{2,0,1:T(8,128)}, f32[8,27,128]{2,0,1:T(8,128)}) async-done(((f32[8,27,128]{2,0,1:T(8,128)}, f32[8,27,128]{2,0,1:T(8,128)}), (f32[8,27,128]{2,0,1:T(8,128)}, f32[8,27,128]{2,0,1:T(8,128)})) %all-reduce.7.cloned.1.call-update) | async-done | bytes 221200 | tf_op jit(solution)/shard_map/psum | solution.py:91
  (317 shorter events, 74.2 us)
Async XLA Ops:
  7.2 193.3 %reduce-scatter.3.cloned.1.call-start = ((), (), s32[]{:S(2)}) async-start(), calls=%async_computation.2 | async-start | bytes 1880064 | tf_op jit(solution)/shard_map/reduce_scatter | solution.py:90
  9.0 83.1 %collective-permute-start.4 = (bf16[1,10,1,32,128]{4,3,2,1,0:T(8,128)(2,1)S(1)}, bf16[1,10,1,32,128]{4,3,2,1,0:T(8,128)(2,1)S(1)}, u32[]{:S(2)}, u32[]{:S(2)}) collective-permute-start(bf16[1,10,1,32,128]{4,3,2,1,0:T(8,128)(2,1)S(1)} %get-tuple-element.114), channel_id=1, source_target_pairs={{0,1},{1,2},{2,3},{3,4},{4,5},{5,6},{6,7},{7,8},{8,9},{9,10},{10,1... | collective-permute-start | bytes 245768 | tf_op jit(solution)/shard_map/ppermute | solution.py:15
  14.4 77.7 %collective-permute-start.5 = (bf16[1,10,1,32,128]{4,3,2,1,0:T(8,128)(2,1)S(1)}, bf16[1,10,1,32,128]{4,3,2,1,0:T(8,128)(2,1)S(1)}, u32[]{:S(2)}, u32[]{:S(2)}) collective-permute-start(bf16[1,10,1,32,128]{4,3,2,1,0:T(8,128)(2,1)S(1)} %get-tuple-element.115), channel_id=1, source_target_pairs={{1,0},{2,1},{3,2},{4,3},{5,4},{6,5},{7,6},{8,7},{9,8},{10,9},{11,1... | collective-permute-start | bytes 245768 | tf_op jit(solution)/shard_map/ppermute | solution.py:17
  20.1 71.1 %collective-permute-start = (bf16[1,10,1,32,128]{4,3,2,1,0:T(8,128)(2,1)S(1)}, bf16[1,10,1,32,128]{4,3,2,1,0:T(8,128)(2,1)S(1)}, u32[]{:S(2)}, u32[]{:S(2)}) collective-permute-start(bf16[1,10,1,32,128]{4,3,2,1,0:T(8,128)(2,1)S(1)} %get-tuple-element.122), channel_id=1, source_target_pairs={{0,1},{1,2},{2,3},{3,4},{4,5},{5,6},{6,7},{7,8},{8,9},{9,10},{10,1... | collective-permute-start | bytes 245768 | tf_op jit(solution)/shard_map/ppermute | solution.py:15
  22.0 69.1 %collective-permute-start.1 = (bf16[1,10,1,32,128]{4,3,2,1,0:T(8,128)(2,1)S(1)}, bf16[1,10,1,32,128]{4,3,2,1,0:T(8,128)(2,1)S(1)}, u32[]{:S(2)}, u32[]{:S(2)}) collective-permute-start(bf16[1,10,1,32,128]{4,3,2,1,0:T(8,128)(2,1)S(1)} %get-tuple-element.123), channel_id=1, source_target_pairs={{1,0},{2,1},{3,2},{4,3},{5,4},{6,5},{7,6},{8,7},{9,8},{10,9},{11,1... | collective-permute-start | bytes 245768 | tf_op jit(solution)/shard_map/ppermute | solution.py:17
  57.6 29.6 %copy-start.1 = (bf16[128,9,128]{2,0,1:T(8,128)(2,1)}, bf16[128,9,128]{2,0,1:T(8,128)(2,1)S(1)}, u32[]{:S(2)}) copy-start(bf16[128,9,128]{2,0,1:T(8,128)(2,1)S(1)} %get-tuple-element.6) | copy-start | bytes 884740
  57.7 29.6 %copy-start.3 = (bf16[128,9,128]{2,0,1:T(8,128)(2,1)}, bf16[128,9,128]{2,0,1:T(8,128)(2,1)S(1)}, u32[]{:S(2)}) copy-start(bf16[128,9,128]{2,0,1:T(8,128)(2,1)S(1)} %get-tuple-element.7) | copy-start | bytes 884740
  57.7 29.8 %copy-start.5 = (bf16[128,9,128]{2,0,1:T(8,128)(2,1)}, bf16[128,9,128]{2,0,1:T(8,128)(2,1)S(1)}, u32[]{:S(2)}) copy-start(bf16[128,9,128]{2,0,1:T(8,128)(2,1)S(1)} %get-tuple-element.8) | copy-start | bytes 884740
  103.9 26.3 %collective-permute-start.2 = (bf16[1,10,1,32,128]{4,3,2,1,0:T(8,128)(2,1)S(1)}, bf16[1,10,1,32,128]{4,3,2,1,0:T(8,128)(2,1)S(1)}, u32[]{:S(2)}, u32[]{:S(2)}) collective-permute-start(bf16[1,10,1,32,128]{4,3,2,1,0:T(8,128)(2,1)S(1)} %get-tuple-element.118), channel_id=1, source_target_pairs={{0,1},{1,2},{2,3},{3,4},{4,5},{5,6},{6,7},{7,8},{8,9},{9,10},{10,1... | collective-permute-start | bytes 245768 | tf_op jit(solution)/shard_map/ppermute | solution.py:15
  121.1 9.1 %collective-permute-start.3 = (bf16[1,10,1,32,128]{4,3,2,1,0:T(8,128)(2,1)S(1)}, bf16[1,10,1,32,128]{4,3,2,1,0:T(8,128)(2,1)S(1)}, u32[]{:S(2)}, u32[]{:S(2)}) collective-permute-start(bf16[1,10,1,32,128]{4,3,2,1,0:T(8,128)(2,1)S(1)} %get-tuple-element.119), channel_id=1, source_target_pairs={{1,0},{2,1},{3,2},{4,3},{5,4},{6,5},{7,6},{8,7},{9,8},{10,9},{11,1... | collective-permute-start | bytes 245768 | tf_op jit(solution)/shard_map/ppermute | solution.py:17
  124.4 144.5 %reduce-scatter.5.cloned.1.call-start = ((), (), s32[]{:S(2)}) async-start(), calls=%async_computation.3 | async-start | bytes 1880064 | tf_op jit(solution)/shard_map/reduce_scatter | solution.py:90
  124.5 8.9 %collective-permute-start.6 = (bf16[1,10,1,32,128]{4,3,2,1,0:T(8,128)(2,1)S(1)}, bf16[1,10,1,32,128]{4,3,2,1,0:T(8,128)(2,1)S(1)}, u32[]{:S(2)}, u32[]{:S(2)}) collective-permute-start(bf16[1,10,1,32,128]{4,3,2,1,0:T(8,128)(2,1)S(1)} %get-tuple-element.110), channel_id=1, source_target_pairs={{0,1},{1,2},{2,3},{3,4},{4,5},{5,6},{6,7},{7,8},{8,9},{9,10},{10,1... | collective-permute-start | bytes 245768 | tf_op jit(solution)/shard_map/ppermute | solution.py:15
  128.1 5.8 %collective-permute-start.7 = (bf16[1,10,1,32,128]{4,3,2,1,0:T(8,128)(2,1)S(1)}, bf16[1,10,1,32,128]{4,3,2,1,0:T(8,128)(2,1)S(1)}, u32[]{:S(2)}, u32[]{:S(2)}) collective-permute-start(bf16[1,10,1,32,128]{4,3,2,1,0:T(8,128)(2,1)S(1)} %get-tuple-element.111), channel_id=1, source_target_pairs={{1,0},{2,1},{3,2},{4,3},{5,4},{6,5},{7,6},{8,7},{9,8},{10,9},{11,1... | collective-permute-start | bytes 245768 | tf_op jit(solution)/shard_map/ppermute | solution.py:17
  156.1 8.9 %copy-start.35 = (bf16[1,10,2,32,128]{4,3,2,1,0:T(8,128)(2,1)S(1)}, bf16[1,10,2,32,128]{4,3,2,1,0:T(8,128)(2,1)}, u32[]{:S(2)}) copy-start(bf16[1,10,2,32,128]{4,3,2,1,0:T(8,128)(2,1)} %get-tuple-element.70) | copy-start | bytes 491524
  181.9 10.2 %copy-start.32 = (bf16[1,10,2,32,128]{4,3,2,1,0:T(8,128)(2,1)S(1)}, bf16[1,10,2,32,128]{4,3,2,1,0:T(8,128)(2,1)}, u32[]{:S(2)}) copy-start(bf16[1,10,2,32,128]{4,3,2,1,0:T(8,128)(2,1)} %get-tuple-element.28) | copy-start | bytes 491524
  181.9 10.9 %copy-start.31 = (bf16[1,10,2,32,128]{4,3,2,1,0:T(8,128)(2,1)S(1)}, bf16[1,10,2,32,128]{4,3,2,1,0:T(8,128)(2,1)}, u32[]{:S(2)}) copy-start(bf16[1,10,2,32,128]{4,3,2,1,0:T(8,128)(2,1)} %get-tuple-element.27) | copy-start | bytes 491524
  181.9 11.6 %copy-start.30 = (bf16[1,10,2,32,128]{4,3,2,1,0:T(8,128)(2,1)S(1)}, bf16[1,10,2,32,128]{4,3,2,1,0:T(8,128)(2,1)}, u32[]{:S(2)}) copy-start(bf16[1,10,2,32,128]{4,3,2,1,0:T(8,128)(2,1)} %get-tuple-element.19) | copy-start | bytes 491524
  181.9 361.5 %all-reduce.7.cloned.1.call-start = ((), (), s32[]{:S(2)}) async-start(), calls=%async_computation.4 | async-start | bytes 442368 | tf_op jit(solution)/shard_map/psum | solution.py:91
  182.0 11.5 %copy-start.10 = (bf16[640,1152]{1,0:T(8,128)(2,1)S(1)}, bf16[640,1152]{1,0:T(8,128)(2,1)}, u32[]{:S(2)}) copy-start(bf16[640,1152]{1,0:T(8,128)(2,1)} %constant_dynamic-update-slice_fusion.107) | copy-start | bytes 4423684
  182.0 11.6 %copy-start.29 = (bf16[1,10,2,32,128]{4,3,2,1,0:T(8,128)(2,1)S(1)}, bf16[1,10,2,32,128]{4,3,2,1,0:T(8,128)(2,1)}, u32[]{:S(2)}) copy-start(bf16[1,10,2,32,128]{4,3,2,1,0:T(8,128)(2,1)} %get-tuple-element.18) | copy-start | bytes 491524
  183.8 9.9 %copy-start.28 = (bf16[1,10,2,32,128]{4,3,2,1,0:T(8,128)(2,1)S(1)}, bf16[1,10,2,32,128]{4,3,2,1,0:T(8,128)(2,1)}, u32[]{:S(2)}) copy-start(bf16[1,10,2,32,128]{4,3,2,1,0:T(8,128)(2,1)} %get-tuple-element.17) | copy-start | bytes 491524
  185.5 8.2 %copy-start.27 = (bf16[1,10,2,32,128]{4,3,2,1,0:T(8,128)(2,1)S(1)}, bf16[1,10,2,32,128]{4,3,2,1,0:T(8,128)(2,1)}, u32[]{:S(2)}) copy-start(bf16[1,10,2,32,128]{4,3,2,1,0:T(8,128)(2,1)} %get-tuple-element.16) | copy-start | bytes 491524
  199.9 69.1 %copy-start.12 = (bf16[640,1152]{1,0:T(8,128)(2,1)S(1)}, bf16[640,1152]{1,0:T(8,128)(2,1)}, u32[]{:S(2)}) copy-start(bf16[640,1152]{1,0:T(8,128)(2,1)} %copy-done.11) | copy-start | bytes 4423684
  199.9 69.1 %copy-start.14 = (bf16[128,9,128]{0,2,1:T(8,128)(2,1)S(1)}, bf16[128,9,128]{0,2,1:T(8,128)(2,1)}, u32[]{:S(2)}) copy-start(bf16[128,9,128]{0,2,1:T(8,128)(2,1)} %copy.72) | copy-start | bytes 884740
  (53 other events, 116.8 us)
Sparse Core Ops, SparseCore 0:
  124.5 69.2 reduce-scatter.2
  196.9 72.0 reduce-scatter.4
  271.9 271.5 all-reduce.6
where the time goes:
time: 554 us; the launch traced here: 553 us
  waiting for transfers between devices  342 us (62%)
  local copies, waits for them, and re-layouts  73.7 us (13%)
  blocking collectives  59.9 us (11%)
  starting transfers between devices  39.4 us (7%)
  between operations  15.2 us (3%)
  matrix products  13 us (2%)
  other arithmetic  9.63 us (2%)
    psum x1, waiting for transfers between devices, reduce_grad(): return lax.psum(owned, 'space')  273 us
    reduce_scatter x2, waiting for transfers between devices, reduce_grad(): owned = lax.psum_scatter(grad_full, 'dp', scatter_dimension=0, tiled=True)  68.5 us
    all_gather x2, blocking collectives, kernel_again(): return lax.all_gather(kernel, 'dp', axis=0, tiled=True)  59.9 us
    unnamed x230, local copies, waits for them, and re-layouts  38.1 us
    ppermute x4, starting transfers between devices, with_halo(): lax.ppermute(tail, axis, [(i, (i + 1) % count) for i in range(ends)])  28.2 us
    reshape x18, local copies, waits for them, and re-layouts, group_window(): pieces.append(piece.reshape(-1, padded.shape[4]))  18.3 us
    ppermute x4, starting transfers between devices, with_halo(): lax.ppermute(head, axis, [((i + 1) % count, i) for i in range(ends)])  11.1 us
  transfers between devices with their start and end apart: 11, of which 3 were waited for; matrix products, arithmetic and copies ran while one was open for 14% of the time, Pallas kernels for 0%

commit v1 on v0

--- a/solution.py
+++ b/solution.py
@@ -88,7 +88,7 @@
 
 def reduce_grad(grad_full):
     owned = lax.psum_scatter(grad_full, "dp", scatter_dimension=0, tiled=True)
-    return lax.psum(owned, "space")
+    return jnp.sum(lax.all_gather(owned, "space"), axis=0)
 
 
 def on_device(inputs, land_mask, weight_one, weight_two, cotangent):

time: 554 us -> 472 us (0.85)
  waiting for transfers between devices: 342 us -> 266 us
  local copies, waits for them, and re-layouts: 73.7 us -> 53.3 us
  starting transfers between devices: 39.4 us -> 50.8 us
    psum x1 -> x0, waiting for transfers between devices: 273 us -> none  [reduce_grad(): return lax.psum(owned, 'space')]
    all_gather x0 -> x2, waiting for transfers between devices: none -> 157 us  [reduce_grad(): return jnp.sum(lax.all_gather(owned, 'space'), axis=0)]
    reduce_scatter x2, waiting for transfers between devices: 68.5 us -> 107 us  [reduce_grad(): owned = lax.psum_scatter(grad_full, 'dp', scatter_dimension=0, tiled=True)]
    unnamed x230 -> x184, local copies, waits for them, and re-layouts: 38.1 us -> 15.6 us
    ppermute x4, starting transfers between devices: 28.2 us -> 39.6 us  [with_halo(): lax.ppermute(tail, axis, [(i, (i + 1) % count) for i in range(ends)])]
    reduce_sum x0 -> x2, other arithmetic: none -> 5.71 us  [reduce_grad(): return jnp.sum(lax.all_gather(owned, 'space'), axis=0)]
  transfers between devices with their start and end apart: 11 -> 12, of which waited for: 3 -> 5; matrix products, arithmetic and copies ran while one was open for 14% -> 12% of each run, Pallas kernels for 0% -> 0%
where the time goes in v1:
time: 472 us; the launch traced here: 471 us
  waiting for transfers between devices  266 us (56%)
  blocking collectives  59.9 us (13%)
  local copies, waits for them, and re-layouts  53.3 us (11%)
  starting transfers between devices  50.8 us (11%)
  between operations  15.2 us (3%)
  other arithmetic  13.7 us (3%)
  matrix products  11.6 us (2%)
    all_gather x2, waiting for transfers between devices, reduce_grad(): return jnp.sum(lax.all_gather(owned, 'space'), axis=0)  157 us
    reduce_scatter x2, waiting for transfers between devices, reduce_grad(): owned = lax.psum_scatter(grad_full, 'dp', scatter_dimension=0, tiled=True)  107 us
    all_gather x2, blocking collectives, kernel_again(): return lax.all_gather(kernel, 'dp', axis=0, tiled=True)  59.9 us
    ppermute x4, starting transfers between devices, with_halo(): lax.ppermute(tail, axis, [(i, (i + 1) % count) for i in range(ends)])  39.6 us
    reshape x18, local copies, waits for them, and re-layouts, group_window(): pieces.append(piece.reshape(-1, padded.shape[4]))  20.2 us
    unnamed x184, local copies, waits for them, and re-layouts  15.6 us
    ppermute x4, starting transfers between devices, with_halo(): lax.ppermute(head, axis, [((i + 1) % count, i) for i in range(ends)])  10.9 us
  transfers between devices with their start and end apart: 12, of which 5 were waited for; matrix products, arithmetic and copies ran while one was open for 12% of the time, Pallas kernels for 0%

profile of v1, /device:TPU:1, one launch (start us, length us, event | category | flops | bytes accessed | tf_op | source)
XLA Modules:
  0.0 470.7 jit_solution(3382744067351547471)
XLA Ops:
  9.0 5.4 %collective-permute-start.4 = (bf16[1,10,1,32,128]{4,3,2,1,0:T(8,128)(2,1)S(1)}, bf16[1,10,1,32,128]{4,3,2,1,0:T(8,128)(2,1)S(1)}, u32[]{:S(2)}, u32[]{:S(2)}) collective-permute-start(bf16[1,10,1,32,128]{4,3,2,1,0:T(8,128)(2,1)S(1)} %get-tuple-element.112), channel_id=1, source_target_pairs={{0,1},{1,2},{2,3},{3,4},{4,5},{5,6},{6,7},{7,8},{8,9},{9,10},{10,1... | collective-permute-start | bytes 245768 | tf_op jit(solution)/shard_map/ppermute | solution.py:15
  14.4 4.7 collective-permute-start.5
  20.1 1.9 collective-permute-start
  22.0 2.4 collective-permute-start.1
  26.2 31.4 %all_gather.21 = bf16[128,27,128]{2,0,1:T(8,128)(2,1)S(1)} all-gather(bf16[8,27,128]{2,0,1:T(8,128)(2,1)S(1)} %convert_element_type.56), channel_id=1, replica_groups=mesh['dp'=16,'space'=32] {'dp'}, dimensions={0}, use_global_device_ids=true | all-gather | bytes 940032 | tf_op jit(solution)/shard_map/all_gather | solution.py:86
  57.7 28.5 %all_gather.20 = bf16[128,27,128]{2,0,1:T(8,128)(2,1)S(1)} all-gather(bf16[8,27,128]{2,0,1:T(8,128)(2,1)S(1)} %convert_element_type.54), channel_id=1, replica_groups=mesh['dp'=16,'space'=32] {'dp'}, dimensions={0}, use_global_device_ids=true | all-gather | bytes 940032 | tf_op jit(solution)/shard_map/all_gather | solution.py:86
  105.0 17.2 %collective-permute-start.2 = (bf16[1,10,1,32,128]{4,3,2,1,0:T(8,128)(2,1)S(1)}, bf16[1,10,1,32,128]{4,3,2,1,0:T(8,128)(2,1)S(1)}, u32[]{:S(2)}, u32[]{:S(2)}) collective-permute-start(bf16[1,10,1,32,128]{4,3,2,1,0:T(8,128)(2,1)S(1)} %get-tuple-element.116), channel_id=1, source_target_pairs={{0,1},{1,2},{2,3},{3,4},{4,5},{5,6},{6,7},{7,8},{8,9},{9,10},{10,1... | collective-permute-start | bytes 245768 | tf_op jit(solution)/shard_map/ppermute | solution.py:15
  122.3 1.9 collective-permute-start.3
  125.8 2.2 collective-permute-done.3
  131.0 1.8 copy.53
  132.8 1.7 copy.52
  139.7 1.7 copy.66
  152.6 2.1 copy.73
  163.2 31.8 %reduce-scatter.3.cloned.1.call-done = f32[8,27,128]{2,0,1:T(8,128)} async-done(((f32[128,27,128]{2,0,1:T(8,128)}), f32[8,27,128]{2,0,1:T(8,128)}) %reduce-scatter.3.cloned.1.call-update) | async-done | bytes 110608 | tf_op jit(solution)/shard_map/reduce_scatter | solution.py:90
  195.0 75.1 %reduce-scatter.5.cloned.1.call-done = f32[8,27,128]{2,0,1:T(8,128)} async-done(((f32[128,27,128]{2,0,1:T(8,128)}), f32[8,27,128]{2,0,1:T(8,128)}) %reduce-scatter.5.cloned.1.call-update) | async-done | bytes 110608 | tf_op jit(solution)/shard_map/reduce_scatter | solution.py:90
  270.2 15.0 %collective-permute-start.6 = (bf16[1,10,1,32,128]{4,3,2,1,0:T(8,128)(2,1)S(1)}, bf16[1,10,1,32,128]{4,3,2,1,0:T(8,128)(2,1)S(1)}, u32[]{:S(2)}, u32[]{:S(2)}) collective-permute-start(bf16[1,10,1,32,128]{4,3,2,1,0:T(8,128)(2,1)S(1)} %get-tuple-element.108), channel_id=1, source_target_pairs={{0,1},{1,2},{2,3},{3,4},{4,5},{5,6},{6,7},{7,8},{8,9},{9,10},{10,1... | collective-permute-start | bytes 245768 | tf_op jit(solution)/shard_map/ppermute | solution.py:15
  285.2 1.9 collective-permute-start.7
  287.1 1.9 copy.72
  289.0 1.9 copy.71
  290.8 1.9 copy.70
  301.6 70.1 %all-gather.5.cloned.1.call-done = f32[256,27,128]{2,0,1:T(8,128)} async-done(((f32[8,27,128]{2,0,1:T(8,128)}), f32[256,27,128]{2,0,1:T(8,128)}) %all-gather.5.cloned.1.call-update) | async-done | bytes 3538960 | tf_op jit(solution)/shard_map/all_gather | solution.py:91
  371.6 2.9 bitcast_reduce_fusion.1
  374.5 86.9 %all-gather.7.cloned.1.call-done = f32[256,27,128]{2,0,1:T(8,128)} async-done(((f32[8,27,128]{2,0,1:T(8,128)}), f32[256,27,128]{2,0,1:T(8,128)}) %all-gather.7.cloned.1.call-update) | async-done | bytes 3538960 | tf_op jit(solution)/shard_map/all_gather | solution.py:91
  461.3 2.9 bitcast_reduce_fusion
  (276 shorter events, 60.4 us)
Async XLA Ops:
  7.2 187.8 %reduce-scatter.3.cloned.1.call-start = ((), (), s32[]{:S(2)}) async-start(), calls=%async_computation.2 | async-start | bytes 1880064 | tf_op jit(solution)/shard_map/reduce_scatter | solution.py:90
  9.0 83.1 %collective-permute-start.4 = (bf16[1,10,1,32,128]{4,3,2,1,0:T(8,128)(2,1)S(1)}, bf16[1,10,1,32,128]{4,3,2,1,0:T(8,128)(2,1)S(1)}, u32[]{:S(2)}, u32[]{:S(2)}) collective-permute-start(bf16[1,10,1,32,128]{4,3,2,1,0:T(8,128)(2,1)S(1)} %get-tuple-element.112), channel_id=1, source_target_pairs={{0,1},{1,2},{2,3},{3,4},{4,5},{5,6},{6,7},{7,8},{8,9},{9,10},{10,1... | collective-permute-start | bytes 245768 | tf_op jit(solution)/shard_map/ppermute | solution.py:15
  14.4 77.7 %collective-permute-start.5 = (bf16[1,10,1,32,128]{4,3,2,1,0:T(8,128)(2,1)S(1)}, bf16[1,10,1,32,128]{4,3,2,1,0:T(8,128)(2,1)S(1)}, u32[]{:S(2)}, u32[]{:S(2)}) collective-permute-start(bf16[1,10,1,32,128]{4,3,2,1,0:T(8,128)(2,1)S(1)} %get-tuple-element.113), channel_id=1, source_target_pairs={{1,0},{2,1},{3,2},{4,3},{5,4},{6,5},{7,6},{8,7},{9,8},{10,9},{11,1... | collective-permute-start | bytes 245768 | tf_op jit(solution)/shard_map/ppermute | solution.py:17
  20.1 69.9 %collective-permute-start = (bf16[1,10,1,32,128]{4,3,2,1,0:T(8,128)(2,1)S(1)}, bf16[1,10,1,32,128]{4,3,2,1,0:T(8,128)(2,1)S(1)}, u32[]{:S(2)}, u32[]{:S(2)}) collective-permute-start(bf16[1,10,1,32,128]{4,3,2,1,0:T(8,128)(2,1)S(1)} %get-tuple-element.120), channel_id=1, source_target_pairs={{0,1},{1,2},{2,3},{3,4},{4,5},{5,6},{6,7},{7,8},{8,9},{9,10},{10,1... | collective-permute-start | bytes 245768 | tf_op jit(solution)/shard_map/ppermute | solution.py:15
  22.0 68.0 %collective-permute-start.1 = (bf16[1,10,1,32,128]{4,3,2,1,0:T(8,128)(2,1)S(1)}, bf16[1,10,1,32,128]{4,3,2,1,0:T(8,128)(2,1)S(1)}, u32[]{:S(2)}, u32[]{:S(2)}) collective-permute-start(bf16[1,10,1,32,128]{4,3,2,1,0:T(8,128)(2,1)S(1)} %get-tuple-element.121), channel_id=1, source_target_pairs={{1,0},{2,1},{3,2},{4,3},{5,4},{6,5},{7,6},{8,7},{9,8},{10,9},{11,1... | collective-permute-start | bytes 245768 | tf_op jit(solution)/shard_map/ppermute | solution.py:17
  57.7 30.5 %copy-start.3 = (bf16[128,9,128]{2,0,1:T(8,128)(2,1)}, bf16[128,9,128]{2,0,1:T(8,128)(2,1)S(1)}, u32[]{:S(2)}) copy-start(bf16[128,9,128]{2,0,1:T(8,128)(2,1)S(1)} %get-tuple-element.4) | copy-start | bytes 884740
  57.7 30.5 %copy-start.5 = (bf16[128,9,128]{2,0,1:T(8,128)(2,1)}, bf16[128,9,128]{2,0,1:T(8,128)(2,1)S(1)}, u32[]{:S(2)}) copy-start(bf16[128,9,128]{2,0,1:T(8,128)(2,1)S(1)} %get-tuple-element.5) | copy-start | bytes 884740
  57.7 31.4 %copy-start.8 = (bf16[128,9,128]{2,0,1:T(8,128)(2,1)}, bf16[128,9,128]{2,0,1:T(8,128)(2,1)S(1)}, u32[]{:S(2)}) copy-start(bf16[128,9,128]{2,0,1:T(8,128)(2,1)S(1)} %get-tuple-element.6) | copy-start | bytes 884740
  86.2 4.4 copy-start.11
  105.0 20.8 %collective-permute-start.2 = (bf16[1,10,1,32,128]{4,3,2,1,0:T(8,128)(2,1)S(1)}, bf16[1,10,1,32,128]{4,3,2,1,0:T(8,128)(2,1)S(1)}, u32[]{:S(2)}, u32[]{:S(2)}) collective-permute-start(bf16[1,10,1,32,128]{4,3,2,1,0:T(8,128)(2,1)S(1)} %get-tuple-element.116), channel_id=1, source_target_pairs={{0,1},{1,2},{2,3},{3,4},{4,5},{5,6},{6,7},{7,8},{8,9},{9,10},{10,1... | collective-permute-start | bytes 245768 | tf_op jit(solution)/shard_map/ppermute | solution.py:15
  122.3 5.8 %collective-permute-start.3 = (bf16[1,10,1,32,128]{4,3,2,1,0:T(8,128)(2,1)S(1)}, bf16[1,10,1,32,128]{4,3,2,1,0:T(8,128)(2,1)S(1)}, u32[]{:S(2)}, u32[]{:S(2)}) collective-permute-start(bf16[1,10,1,32,128]{4,3,2,1,0:T(8,128)(2,1)S(1)} %get-tuple-element.117), channel_id=1, source_target_pairs={{1,0},{2,1},{3,2},{4,3},{5,4},{6,5},{7,6},{8,7},{9,8},{10,9},{11,1... | collective-permute-start | bytes 245768 | tf_op jit(solution)/shard_map/ppermute | solution.py:17
  125.6 144.5 %reduce-scatter.5.cloned.1.call-start = ((), (), s32[]{:S(2)}) async-start(), calls=%async_computation.3 | async-start | bytes 1880064 | tf_op jit(solution)/shard_map/reduce_scatter | solution.py:90
  131.0 10.4 %copy-start.20 = (bf16[1,10,2,32,128]{4,3,2,1,0:T(8,128)(2,1)S(1)}, bf16[1,10,2,32,128]{4,3,2,1,0:T(8,128)(2,1)}, u32[]{:S(2)}) copy-start(bf16[1,10,2,32,128]{4,3,2,1,0:T(8,128)(2,1)} %get-tuple-element.59) | copy-start | bytes 491524
  131.0 11.2 %copy-start.19 = (bf16[1,10,2,32,128]{4,3,2,1,0:T(8,128)(2,1)S(1)}, bf16[1,10,2,32,128]{4,3,2,1,0:T(8,128)(2,1)}, u32[]{:S(2)}) copy-start(bf16[1,10,2,32,128]{4,3,2,1,0:T(8,128)(2,1)} %get-tuple-element.60) | copy-start | bytes 491524
  131.0 12.0 %copy-start.18 = (bf16[1,10,2,32,128]{4,3,2,1,0:T(8,128)(2,1)S(1)}, bf16[1,10,2,32,128]{4,3,2,1,0:T(8,128)(2,1)}, u32[]{:S(2)}) copy-start(bf16[1,10,2,32,128]{4,3,2,1,0:T(8,128)(2,1)} %get-tuple-element.61) | copy-start | bytes 491524
  152.6 5.2 %copy-start.28 = (bf16[640,128]{0,1:T(8,128)(2,1)S(1)}, bf16[640,128]{0,1:T(8,128)(2,1)}, u32[]{:S(2)}) copy-start(bf16[640,128]{0,1:T(8,128)(2,1)} %copy.52) | copy-start | bytes 491524
  154.7 3.2 copy-start.34
  154.7 3.3 copy-start.33
  154.7 3.3 copy-start.31
  154.7 3.3 copy-start.30
  163.1 208.5 %all-gather.5.cloned.1.call-start = ((), (), s32[]{:S(2)}) async-start(), calls=%async_computation.4 | async-start | bytes 3649536 | tf_op jit(solution)/shard_map/all_gather | solution.py:91
  195.0 266.4 %all-gather.7.cloned.1.call-start = ((), (), s32[]{:S(2)}) async-start(), calls=%async_computation.5 | async-start | bytes 3649536 | tf_op jit(solution)/shard_map/all_gather | solution.py:91
  270.2 22.5 %collective-permute-start.6 = (bf16[1,10,1,32,128]{4,3,2,1,0:T(8,128)(2,1)S(1)}, bf16[1,10,1,32,128]{4,3,2,1,0:T(8,128)(2,1)S(1)}, u32[]{:S(2)}, u32[]{:S(2)}) collective-permute-start(bf16[1,10,1,32,128]{4,3,2,1,0:T(8,128)(2,1)S(1)} %get-tuple-element.108), channel_id=1, source_target_pairs={{0,1},{1,2},{2,3},{3,4},{4,5},{5,6},{6,7},{7,8},{8,9},{9,10},{10,1... | collective-permute-start | bytes 245768 | tf_op jit(solution)/shard_map/ppermute | solution.py:15
  285.2 7.5 %collective-permute-start.7 = (bf16[1,10,1,32,128]{4,3,2,1,0:T(8,128)(2,1)S(1)}, bf16[1,10,1,32,128]{4,3,2,1,0:T(8,128)(2,1)S(1)}, u32[]{:S(2)}, u32[]{:S(2)}) collective-permute-start(bf16[1,10,1,32,128]{4,3,2,1,0:T(8,128)(2,1)S(1)} %get-tuple-element.109), channel_id=1, source_target_pairs={{1,0},{2,1},{3,2},{4,3},{5,4},{6,5},{7,6},{8,7},{9,8},{10,9},{11,1... | collective-permute-start | bytes 245768 | tf_op jit(solution)/shard_map/ppermute | solution.py:17
  (32 other events, 40.4 us)
Sparse Core Ops, SparseCore 0:
  125.7 69.1 reduce-scatter.2
  198.0 72.0 reduce-scatter.4
  273.3 98.2 all-gather.4
  374.6 86.6 all-gather.6
